TPU v7x, 128 devices: a whole 4x4x4 slice. The times are simulated.
128 devices in a mesh: row: 8 (over z_lo, y), col: 16 (over x, z_hi, core).
Axes of the slice: x: 4, y: 4, z: 4 (z_hi: 2, z_lo: 2; z = z_hi * 2 + z_lo), core: 2. Of those that a mesh axis runs over, the one named last changes fastest.
Arguments:
- factors: bfloat16 [10240, 3, 2048], P(('row', 'col')), may hold values from -0.59765625 to 0.59765625
- occ_energy: float32 [300], replicated, may hold values from -3 to -0.5
- vir_energy: float32 [2048], replicated, may hold values from 0.3 to 4
- slab_orbitals: int32 [3], replicated, may hold values from 0 to 299
- pair_list: int32 [16, 2], replicated, may hold values from 0 to 2
- pair_state: int32 [16], replicated, may hold values from 0 to 3
- state_shift: float32 [4], replicated, may hold values from 0.1 to 1
Outputs:
- amplitudes: float32 [16, 2048, 2048], P(None, 'row', 'col')
All inputs are finite; a program needn't handle non-finite values.
Results may differ from a plain program's by a relative error of at most 0.0003.
Values may be sent and summed in bfloat16 or wider, within the bound.
No kernel may reach another device: no remote copies, remote signals or barrier semaphores. Data moves between devices by JAX's collectives and lax.ppermute only.
A program may use at most 192 MiB of HBM per device.

v0:
```python
import jax
import jax.numpy as jnp
from jax import lax
from jax.sharding import Mesh, PartitionSpec as P


def row_ring(n_row):
    half = n_row // 2
    return list(range(half)) + [half + y for y in reversed(range(half))]


def ring_gather(shard, axis, ring):
    n = len(ring)
    position = [0] * n
    for k, r in enumerate(ring):
        position[r] = k
    right = [(ring[k], ring[(k + 1) % n]) for k in range(n)]
    left = [(ring[k], ring[(k - 1) % n]) for k in range(n)]
    ring_arr = jnp.array(ring, dtype=jnp.int32)
    me = lax.axis_index(axis)
    my_pos = jnp.array(position, dtype=jnp.int32)[me]
    out = jnp.zeros((n,) + shard.shape, shard.dtype)
    out = lax.dynamic_update_index_in_dim(out, shard, me, 0)
    go_right = go_left = shard
    n_right = n // 2
    n_left = n - 1 - n_right
    for step in range(1, n_right + 1):
        go_right = lax.ppermute(go_right, axis, right)
        out = lax.dynamic_update_index_in_dim(out, go_right, ring_arr[(my_pos - step) % n], 0)
        if step <= n_left:
            go_left = lax.ppermute(go_left, axis, left)
            out = lax.dynamic_update_index_in_dim(out, go_left, ring_arr[(my_pos + step) % n], 0)
    return out


def shards(factors, occ_energy, vir_energy, slab_orbitals, pair_list, pair_state, state_shift):
    n_row = lax.axis_size("row")
    n_colx = lax.axis_size("colx")
    n_core = lax.axis_size("core")
    n_col = n_colx * n_core
    local_aux, nocc, nvir = factors.shape
    rows_a = nvir // n_row
    cols_b = nvir // n_col
    spread_a = lax.all_to_all(
        factors.reshape(local_aux, nocc, n_row, rows_a),
        "row",
        split_axis=2,
        concat_axis=0,
        tiled=True,
    ).reshape(n_row * local_aux, nocc, rows_a)
    half_a = lax.all_gather(spread_a, "colx", axis=0, tiled=True)
    other_a = lax.ppermute(half_a, "core", [(k, (k + 1) % n_core) for k in range(n_core)])
    spread_b = lax.all_to_all(
        factors.reshape(local_aux, nocc, n_col, cols_b),
        ("colx", "core"),
        split_axis=2,
        concat_axis=0,
        tiled=True,
    ).reshape(n_col * local_aux, nocc, cols_b)
    block_b = ring_gather(spread_b, "row", row_ring(n_row))
    block_b = block_b.reshape(n_row, n_colx, n_core, local_aux, nocc, cols_b)
    me_core = lax.axis_index("core")
    contract = "xrpia,rxpjb->ijab"
    gram = jnp.einsum(
        contract,
        half_a.reshape(n_colx, n_row, local_aux, nocc, rows_a),
        lax.dynamic_index_in_dim(block_b, me_core, 2, keepdims=False),
        preferred_element_type=jnp.float32,
    ) + jnp.einsum(
        contract,
        other_a.reshape(n_colx, n_row, local_aux, nocc, rows_a),
        lax.dynamic_index_in_dim(block_b, (me_core + n_core - 1) % n_core, 2, keepdims=False),
        preferred_element_type=jnp.float32,
    )
    gram = gram.reshape(nocc * nocc, rows_a, cols_b)
    first = pair_list[:, 0]
    second = pair_list[:, 1]
    kernel = jnp.take(gram, first * nocc + second, axis=0)
    vir_a = lax.dynamic_slice_in_dim(vir_energy, lax.axis_index("row") * rows_a, rows_a)
    col_index = lax.axis_index("colx") * n_core + me_core
    vir_b = lax.dynamic_slice_in_dim(vir_energy, col_index * cols_b, cols_b)
    e_first = occ_energy[slab_orbitals[first]]
    e_second = occ_energy[slab_orbitals[second]]
    shift = state_shift[pair_state]
    denom = (
        vir_a[None, :, None]
        + vir_b[None, None, :]
        - e_first[:, None, None]
        - e_second[:, None, None]
        + shift[:, None, None]
    )
    return -kernel / denom


def solution(mesh):
    n_row, n_col = mesh.devices.shape
    sub = Mesh(mesh.devices.reshape(n_row, n_col // 2, 2), ("row", "colx", "core"))
    placed = (P(("row", "colx", "core"), None, None), P(), P(), P(), P(), P(), P())
    return jax.shard_map(
        shards,
        mesh=sub,
        in_specs=placed,
        out_specs=P(None, "row", ("colx", "core")),
        check_vma=False,
    )
```

profile of v0, /device:TPU:0, one launch (start us, length us, event | category | flops | bytes accessed | tf_op | source)
XLA Modules:
  0.0 275.2 jit_solution(11836928373755230479)
XLA Ops:
  6.5 0.0 copy-start
  6.5 0.0 copy-start.2
  6.5 0.0 all-gather.2.cloned.1.call-start
  6.5 1.4 copy.72
  7.9 20.7 %all_to_all.30 = bf16[80,3,8,256]{3,0,1,2:T(8,128)(2,1)S(1)} all-to-all(bf16[80,3,8,256]{3,0,1,2:T(8,128)(2,1)S(1)} %bitcast.118), channel_id=1, replica_groups=mesh['row'=8,'colx'=8,'core'=2] {'row'}, dimensions={2} | all-to-all | bytes 1966080 | tf_op jit(solution)/shard_map/all_to_all | solution.py:44
  28.6 0.0 copy-start.4
  28.6 0.0 copy-start.6
  28.6 0.0 copy-start.5
  28.6 1.0 copy.27
  29.7 0.0 all-gather.2.cloned.1.call-update
  29.7 0.0 copy-start.1
  29.7 103.7 %all-gather.2.cloned.1.call-done = bf16[5120,3,256]{2,0,1:T(8,128)(2,1)} async-done(((bf16[640,3,256]{2,0,1:T(8,128)(2,1)}), bf16[5120,3,256]{2,0,1:T(8,128)(2,1)}) %all-gather.2.cloned.1.call-update) | async-done | bytes 7864336 | tf_op jit(solution)/shard_map/all_gather | solution.py:51
  133.4 0.0 collective-permute-start.7
  133.4 0.0 copy-done.2
  133.4 1.1 copy_bitcast_fusion.1
  134.5 3.6 %all-to-all-start = ((bf16[80,3,16,128]{3,0,1,2:T(8,128)(2,1)}), bf16[80,3,16,128]{3,0,1,2:T(8,128)(2,1)S(1)}, u32[]{:S(2)}, u32[]{:S(2)}) async-start(bf16[80,3,16,128]{3,0,1,2:T(8,128)(2,1)} %copy_bitcast_fusion.1), calls=%async_computation | async-start | bytes 1966080 | tf_op jit(solution)/shard_map/all_to_all | solution.py:53
  138.2 0.0 copy-done.4
  138.2 0.7 fusion.32
  138.9 0.0 copy-done.6
  138.9 0.0 copy-done.5
  138.9 1.9 fusion.30
  140.8 14.6 %all-to-all-done = bf16[80,3,16,128]{3,0,1,2:T(8,128)(2,1)S(1)} async-done(((bf16[80,3,16,128]{3,0,1,2:T(8,128)(2,1)}), bf16[80,3,16,128]{3,0,1,2:T(8,128)(2,1)S(1)}, u32[]{:S(2)}, u32[]{:S(2)}) %all-to-all-start) | async-done | bytes 983072 | tf_op jit(solution)/shard_map/all_to_all | solution.py:53
  155.4 0.1 copy.24
  155.5 1.6 collective-permute-start
  157.0 0.5 collective-permute-start.1
  157.6 0.0 copy-done.3
  157.6 0.6 dynamic_slice.37
  162.8 0.7 fusion.33
  172.5 0.8 dynamic_slice.48
  173.3 0.8 dynamic_slice.47
  174.0 0.0 copy-done
  174.0 0.7 gather_fusion.1
  174.7 0.7 gather_fusion.2
  179.8 0.0 copy-done.1
  179.9 0.7 gather_fusion.3
  180.5 0.1 broadcast_add_fusion
  180.6 1.7 broadcast_in_dim.51
  182.3 0.1 constant_dynamic-update-slice_fusion
  182.5 0.0 collective-permute-done
  182.5 1.6 collective-permute-start.2
  184.0 0.0 collective-permute-done.1
  184.0 0.5 collective-permute-start.3
  184.6 0.1 bitcast_dynamic-update-slice_fusion.6
  184.7 0.1 bitcast_dynamic-update-slice_fusion.5
  184.9 20.2 %collective-permute-done.2 = bf16[1280,3,128]{2,0,1:T(8,128)(2,1)S(1)} collective-permute-done((bf16[1280,3,128]{2,0,1:T(8,128)(2,1)S(1)}, bf16[1280,3,128]{2,0,1:T(8,128)(2,1)S(1)}, u32[]{:S(2)}, u32[]{:S(2)}) %collective-permute-start.2) | collective-permute-done | bytes 983072 | tf_op jit(solution)/shard_map/ppermute | solution.py:28
  205.0 1.5 collective-permute-start.4
  206.5 0.0 collective-permute-done.3
  206.5 0.5 collective-permute-start.5
  207.0 0.1 bitcast_dynamic-update-slice_fusion.4
  207.2 0.1 bitcast_dynamic-update-slice_fusion.3
  207.3 19.6 %collective-permute-done.4 = bf16[1280,3,128]{2,0,1:T(8,128)(2,1)S(1)} collective-permute-done((bf16[1280,3,128]{2,0,1:T(8,128)(2,1)S(1)}, bf16[1280,3,128]{2,0,1:T(8,128)(2,1)S(1)}, u32[]{:S(2)}, u32[]{:S(2)}) %collective-permute-start.4) | collective-permute-done | bytes 983072 | tf_op jit(solution)/shard_map/ppermute | solution.py:28
  226.9 1.5 collective-permute-start.6
  228.4 0.1 bitcast_dynamic-update-slice_fusion.2
  228.6 0.0 collective-permute-done.5
  228.6 0.1 bitcast_dynamic-update-slice_fusion.1
  228.7 19.0 %collective-permute-done.6 = bf16[1280,3,128]{2,0,1:T(8,128)(2,1)S(1)} collective-permute-done((bf16[1280,3,128]{2,0,1:T(8,128)(2,1)S(1)}, bf16[1280,3,128]{2,0,1:T(8,128)(2,1)S(1)}, u32[]{:S(2)}, u32[]{:S(2)}) %collective-permute-start.6) | collective-permute-done | bytes 983072 | tf_op jit(solution)/shard_map/ppermute | solution.py:28
  247.7 0.1 bitcast_dynamic-update-slice_fusion
  247.8 3.2 %constant_dynamic-slice_fusion.1 = (bf16[8,8,1,80,3,128]{5,3,2,1,4,0:T(8,128)(2,1)S(1)}, bf16[8,8,1,80,3,128]{5,3,2,1,4,0:T(8,128)(2,1)}) fusion(bf16[8,8,2,80,3,128]{5,3,2,1,4,0:T(8,128)(2,1)S(1)} %bitcast.111, s32[]{:T(128)S(6)} %select_n.160, s32[]{:T(128)S(6)} %select_n.162), kind=kLoop, calls=%fused_computation.40 | loop fusion | bytes 15728648 | tf_op jit(solution)/shard_map/jit(dynamic_index_in_dim)/dynamic_slice | solution.py:67
  251.1 0.0 collective-permute-done.7
  251.1 7.7 %fusion.15 = f32[3,128,3,256]{3,1,2,0:T(8,128)S(1)} fusion(bf16[8,8,80,3,256]{4,2,1,0,3:T(8,128)(2,1)} %bitcast.42, bf16[8,8,1,80,3,128]{5,3,2,1,4,0:T(8,128)(2,1)} %get-tuple-element.8), kind=kOutput, calls=%fused_computation.16 | convolution fusion | flops 3019898880 | bytes 12976128 | tf_op jit(solution)/shard_map/xrpia,rxpjb->ijab/dot_general | solution.py:69
  258.8 6.5 %fusion.25 = f32[3,3,256,128]{2,3,0,1:T(8,128)S(1)} fusion(f32[3,128,3,256]{3,1,2,0:T(8,128)S(1)} %fusion.15, bf16[8,8,80,3,256]{4,2,1,0,3:T(8,128)(2,1)} %bitcast.120, bf16[8,8,1,80,3,128]{5,3,2,1,4,0:T(8,128)(2,1)S(1)} %get-tuple-element.7), kind=kOutput, calls=%fused_computation.18 | convolution fusion | flops 3020193792 | bytes 14155776 | tf_op jit(solution)/shard_map/xrpia,rxpjb->ijab/dot_general | solution.py:64
  265.3 0.4 copy.31
  265.7 0.7 gather_fusion
  266.4 1.9 add_divide_fusion
  (6 shorter events, 0.0 us)
Async XLA Ops:
  6.5 167.5 %copy-start = (f32[300]{0:T(512)S(1)}, f32[300]{0:T(512)}, u32[]{:S(2)}) copy-start(f32[300]{0:T(512)} %param.10) | copy-start | bytes 3604
  6.5 126.9 %copy-start.2 = (bf16[80,3,2048]{2,0,1:T(8,128)(2,1)S(1)}, bf16[80,3,2048]{2,0,1:T(8,128)(2,1)}, u32[]{:S(2)}) copy-start(bf16[80,3,2048]{2,0,1:T(8,128)(2,1)} %param.9) | copy-start | bytes 2949124
  6.5 126.9 %all-gather.2.cloned.1.call-start = ((), (), s32[]{:S(2)}) async-start(), calls=%async_computation.2 | async-start | bytes 8847360 | tf_op jit(solution)/shard_map/all_gather | solution.py:51
  28.6 109.6 %copy-start.4 = (s32[3]{0:T(128)S(1)}, s32[3]{0:T(128)}, u32[]{:S(2)}) copy-start(s32[3]{0:T(128)} %param.12) | copy-start | bytes 40
  28.6 110.2 %copy-start.6 = (s32[16]{0:T(128)S(1)}, s32[16]{0:T(128)}, u32[]{:S(2)}) copy-start(s32[16]{0:T(128)} %param.14) | copy-start | bytes 196
  28.6 110.2 %copy-start.5 = (s32[16,2]{0,1:T(2,128)S(1)}, s32[16,2]{0,1:T(2,128)}, u32[]{:S(2)}) copy-start(s32[16,2]{0,1:T(2,128)} %param.13) | copy-start | bytes 388
  29.7 127.9 %copy-start.3 = (s32[8]{0:T(128)S(1)}, s32[8]{0:T(128)}, u32[]{:S(2)}) copy-start(s32[8]{0:T(128)} %constant.138.clone) | copy-start | bytes 100
  29.7 150.2 %copy-start.1 = (f32[4]{0:T(128)S(1)}, f32[4]{0:T(128)}, u32[]{:S(2)}) copy-start(f32[4]{0:T(128)} %param.15) | copy-start | bytes 52
  133.4 117.6 %collective-permute-start.7 = (bf16[5120,3,256]{2,0,1:T(8,128)(2,1)}, bf16[5120,3,256]{2,0,1:T(8,128)(2,1)}, u32[]{:S(2)}, u32[]{:S(2)}) collective-permute-start(bf16[5120,3,256]{2,0,1:T(8,128)(2,1)} %all-gather.2.cloned.1.call-done), channel_id=1, source_target_pairs={{0,1},{1,0},{2,3},{3,2},{4,5},{5,4},{6,7},{7,6},{8,9},{9,8},{10,11... | collective-permute-start | bytes 23592968 | tf_op jit(solution)/shard_map/ppermute | solution.py:52
  134.5 20.9 %all-to-all-start = ((bf16[80,3,16,128]{3,0,1,2:T(8,128)(2,1)}), bf16[80,3,16,128]{3,0,1,2:T(8,128)(2,1)S(1)}, u32[]{:S(2)}, u32[]{:S(2)}) async-start(bf16[80,3,16,128]{3,0,1,2:T(8,128)(2,1)} %copy_bitcast_fusion.1), calls=%async_computation | async-start | bytes 1966080 | tf_op jit(solution)/shard_map/all_to_all | solution.py:53
  155.5 27.0 %collective-permute-start = (bf16[1280,3,128]{2,0,1:T(8,128)(2,1)S(1)}, bf16[1280,3,128]{2,0,1:T(8,128)(2,1)S(1)}, u32[]{:S(2)}, u32[]{:S(2)}) collective-permute-start(bf16[1280,3,128]{2,0,1:T(8,128)(2,1)S(1)} %bitcast.114), channel_id=1, source_target_pairs={{0,16},{16,32},{32,48},{48,112},{112,96},{96,80},{80,64},{64,0},{1... | collective-permute-start | bytes 2949128 | tf_op jit(solution)/shard_map/ppermute | solution.py:28
  157.0 27.0 %collective-permute-start.1 = (bf16[1280,3,128]{2,0,1:T(8,128)(2,1)S(1)}, bf16[1280,3,128]{2,0,1:T(8,128)(2,1)S(1)}, u32[]{:S(2)}, u32[]{:S(2)}) collective-permute-start(bf16[1280,3,128]{2,0,1:T(8,128)(2,1)S(1)} %bitcast.115), channel_id=1, source_target_pairs={{0,64},{16,0},{32,16},{48,32},{112,48},{96,112},{80,96},{64,80},{1... | collective-permute-start | bytes 2949128 | tf_op jit(solution)/shard_map/ppermute | solution.py:31
  182.5 22.5 %collective-permute-start.2 = (bf16[1280,3,128]{2,0,1:T(8,128)(2,1)S(1)}, bf16[1280,3,128]{2,0,1:T(8,128)(2,1)S(1)}, u32[]{:S(2)}, u32[]{:S(2)}) collective-permute-start(bf16[1280,3,128]{2,0,1:T(8,128)(2,1)S(1)} %collective-permute-done), channel_id=1, source_target_pairs={{0,16},{16,32},{32,48},{48,112},{112,96},{96,80},{80,64},{64,0},{1... | collective-permute-start | bytes 2949128 | tf_op jit(solution)/shard_map/ppermute | solution.py:28
  184.0 22.5 %collective-permute-start.3 = (bf16[1280,3,128]{2,0,1:T(8,128)(2,1)S(1)}, bf16[1280,3,128]{2,0,1:T(8,128)(2,1)S(1)}, u32[]{:S(2)}, u32[]{:S(2)}) collective-permute-start(bf16[1280,3,128]{2,0,1:T(8,128)(2,1)S(1)} %collective-permute-done.1), channel_id=1, source_target_pairs={{0,64},{16,0},{32,16},{48,32},{112,48},{96,112},{80,96},{64,80},{1... | collective-permute-start | bytes 2949128 | tf_op jit(solution)/shard_map/ppermute | solution.py:31
  205.0 21.9 %collective-permute-start.4 = (bf16[1280,3,128]{2,0,1:T(8,128)(2,1)S(1)}, bf16[1280,3,128]{2,0,1:T(8,128)(2,1)S(1)}, u32[]{:S(2)}, u32[]{:S(2)}) collective-permute-start(bf16[1280,3,128]{2,0,1:T(8,128)(2,1)S(1)} %collective-permute-done.2), channel_id=1, source_target_pairs={{0,16},{16,32},{32,48},{48,112},{112,96},{96,80},{80,64},{64,0},{1... | collective-permute-start | bytes 2949128 | tf_op jit(solution)/shard_map/ppermute | solution.py:28
  206.5 22.1 %collective-permute-start.5 = (bf16[1280,3,128]{2,0,1:T(8,128)(2,1)S(1)}, bf16[1280,3,128]{2,0,1:T(8,128)(2,1)S(1)}, u32[]{:S(2)}, u32[]{:S(2)}) collective-permute-start(bf16[1280,3,128]{2,0,1:T(8,128)(2,1)S(1)} %collective-permute-done.3), channel_id=1, source_target_pairs={{0,64},{16,0},{32,16},{48,32},{112,48},{96,112},{80,96},{64,80},{1... | collective-permute-start | bytes 2949128 | tf_op jit(solution)/shard_map/ppermute | solution.py:31
  226.9 20.8 %collective-permute-start.6 = (bf16[1280,3,128]{2,0,1:T(8,128)(2,1)S(1)}, bf16[1280,3,128]{2,0,1:T(8,128)(2,1)S(1)}, u32[]{:S(2)}, u32[]{:S(2)}) collective-permute-start(bf16[1280,3,128]{2,0,1:T(8,128)(2,1)S(1)} %collective-permute-done.4), channel_id=1, source_target_pairs={{0,16},{16,32},{32,48},{48,112},{112,96},{96,80},{80,64},{64,0},{1... | collective-permute-start | bytes 2949128 | tf_op jit(solution)/shard_map/ppermute | solution.py:28
Sparse Core Ops, SparseCore 0:
  29.8 103.5 all-gather.1
where the time goes:
time: 276 us; the launch traced here: 275 us
  waiting for transfers between devices  177 us (64%)
  between operations  31.7 us (11%)
  blocking collectives  20.7 us (8%)
  local copies, waits for them, and re-layouts  16 us (6%)
  matrix products  14.2 us (5%)
  starting transfers between devices  11.4 us (4%)
  other arithmetic  4.01 us (1%)
    all_gather x1, waiting for transfers between devices, shards(): half_a = lax.all_gather(spread_a, 'colx', axis=0, tiled=True)  104 us
    ppermute x4, waiting for transfers between devices, ring_gather(): go_right = lax.ppermute(go_right, axis, right)  58.8 us
    all_to_all x1, blocking collectives, shards(): lax.all_to_all(factors.reshape(local_aux, nocc, n_row, rows_a), 'row', sp...  20.7 us
    all_to_all x1, waiting for transfers between devices, shards(): lax.all_to_all(factors.reshape(local_aux, nocc, n_col, cols_b), ('colx',...  14.6 us
    dot_general x1, matrix products, shards(): jnp.einsum(contract, other_a.reshape(n_colx, n_row, local_aux, nocc, rows...  7.69 us
    dot_general x1, matrix products, shards(): jnp.einsum(contract, half_a.reshape(n_colx, n_row, local_aux, nocc, rows_...  6.54 us
    ppermute x4, starting transfers between devices, ring_gather(): go_right = lax.ppermute(go_right, axis, right)  6.08 us
  transfers between devices with their start and end apart: 10, of which 5 were waited for; matrix products, arithmetic and copies ran while one was open for 5% of the time, Pallas kernels for 0%

commit v1 on v0

--- a/solution.py
+++ b/solution.py
@@ -1,7 +1,18 @@
+import functools
 import jax
 import jax.numpy as jnp
 from jax import lax
 from jax.sharding import Mesh, PartitionSpec as P
+
+
+def state_rails_now(content, ndim_at):
+    earlier = lax.axis_size("colx")
+    kept_arr = jnp.stack([content] * earlier, 0)
+    extra = lax.all_to_all(kept_arr, "colx", 0, 0)
+    return jnp.concatenate(extra, ndim_at)
+
+
+fit_goods_all = functools.partial(state_rails_now, ndim_at=0)
 
 
 def row_ring(n_row):
@@ -48,7 +59,7 @@
         concat_axis=0,
         tiled=True,
     ).reshape(n_row * local_aux, nocc, rows_a)
-    half_a = lax.all_gather(spread_a, "colx", axis=0, tiled=True)
+    half_a = fit_goods_all(spread_a)
     other_a = lax.ppermute(half_a, "core", [(k, (k + 1) % n_core) for k in range(n_core)])
     spread_b = lax.all_to_all(
         factors.reshape(local_aux, nocc, n_col, cols_b),

time: 276 us -> 259 us (0.938)
  waiting for transfers between devices: 177 us -> 73.7 us
  blocking collectives: 20.7 us -> 117 us
  between operations: 31.7 us -> 18.1 us
  local copies, waits for them, and re-layouts: 16 us -> 22.6 us
    all_gather x1 -> x0, waiting for transfers between devices: 104 us -> none  [shards(): half_a = lax.all_gather(spread_a, 'colx', axis=0, tiled=True)]
    all_to_all x0 -> x1, blocking collectives: none -> 96 us  [state_rails_now(): extra = lax.all_to_all(kept_arr, 'colx', 0, 0)]
    all_to_all x0 -> x1, local copies, waits for them, and re-layouts: none -> 3.89 us  [state_rails_now(): extra = lax.all_to_all(kept_arr, 'colx', 0, 0)]
  transfers between devices with their start and end apart: 10 -> 9, of which waited for: 5 -> 4; matrix products, arithmetic and copies ran while one was open for 5% -> 6% of each run, Pallas kernels for 0% -> 0%
where the time goes in v1:
time: 259 us; the launch traced here: 258 us
  blocking collectives  117 us (45%)
  waiting for transfers between devices  73.7 us (28%)
  local copies, waits for them, and re-layouts  22.6 us (9%)
  between operations  18.1 us (7%)
  matrix products  12.2 us (5%)
  starting transfers between devices  11.2 us (4%)
  other arithmetic  3.87 us (1%)
    all_to_all x1, blocking collectives, state_rails_now(): extra = lax.all_to_all(kept_arr, 'colx', 0, 0)  96 us
    ppermute x4, waiting for transfers between devices, ring_gather(): go_right = lax.ppermute(go_right, axis, right)  58.9 us
    all_to_all x1, blocking collectives, shards(): lax.all_to_all(factors.reshape(local_aux, nocc, n_row, rows_a), 'row', sp...  20.7 us
    all_to_all x1, waiting for transfers between devices, shards(): lax.all_to_all(factors.reshape(local_aux, nocc, n_col, cols_b), ('colx',...  14.8 us
    dot_general x1, matrix products, shards(): jnp.einsum(contract, other_a.reshape(n_colx, n_row, local_aux, nocc, rows...  7.83 us
    ppermute x4, starting transfers between devices, ring_gather(): go_right = lax.ppermute(go_right, axis, right)  5.44 us
  transfers between devices with their start and end apart: 9, of which 4 were waited for; matrix products, arithmetic and copies ran while one was open for 6% of the time, Pallas kernels for 0%

profile of v1, /device:TPU:0, one launch (start us, length us, event | category | flops | bytes accessed | tf_op | source)
XLA Modules:
  0.0 258.4 jit_solution(5902699984389085488)
XLA Ops:
  0.0 0.0 copy-start
  0.0 1.3 copy.74
  1.3 20.7 %all_to_all.35 = bf16[80,3,8,256]{3,0,1,2:T(8,128)(2,1)S(1)} all-to-all(bf16[80,3,8,256]{3,0,1,2:T(8,128)(2,1)S(1)} %bitcast.123), channel_id=1, replica_groups=mesh['row'=8,'colx'=8,'core'=2] {'row'}, dimensions={2} | all-to-all | bytes 1966080 | tf_op jit(solution)/shard_map/all_to_all | solution.py:55
  22.0 0.1 copy.28
  22.1 0.8 stack.3
  22.9 96.0 %all_to_all.36 = bf16[8,640,3,256]{3,1,2,0:T(8,128)(2,1)S(1)} all-to-all(bf16[8,640,3,256]{3,1,2,0:T(8,128)(2,1)S(1)} %stack.3), channel_id=1, replica_groups=mesh['row'=8,'colx'=8,'core'=2] {'colx'}, dimensions={0} | all-to-all | bytes 15728640 | tf_op jit(solution)/shard_map/all_to_all | solution.py:11
  119.0 0.0 copy-start.7
  119.0 0.0 copy-start.5
  119.0 0.0 copy-start.2
  119.0 3.9 %copy.31 = bf16[8,640,3,256]{3,1,0,2:T(8,128)(2,1)} copy(bf16[8,640,3,256]{3,1,2,0:T(8,128)(2,1)S(1)} %all_to_all.36) | data formatting | bytes 15728640 | tf_op jit(solution)/shard_map/all_to_all | solution.py:11
  122.9 1.5 copy-done.3
  124.4 0.0 collective-permute-start.7
  124.4 0.0 copy-done.4
  124.4 1.1 copy_bitcast_fusion.1
  125.5 3.6 %all-to-all-start = ((bf16[80,3,16,128]{3,0,1,2:T(8,128)(2,1)}), bf16[80,3,16,128]{3,0,1,2:T(8,128)(2,1)S(1)}, u32[]{:S(2)}, u32[]{:S(2)}) async-start(bf16[80,3,16,128]{3,0,1,2:T(8,128)(2,1)} %copy_bitcast_fusion.1), calls=%async_computation | async-start | bytes 1966080 | tf_op jit(solution)/shard_map/all_to_all | solution.py:64
  129.2 0.0 copy-done.6
  129.2 0.6 fusion.32
  129.8 0.0 copy-done.8
  129.8 0.0 copy-done.7
  129.8 1.8 fusion.30
  131.6 14.8 %all-to-all-done = bf16[80,3,16,128]{3,0,1,2:T(8,128)(2,1)S(1)} async-done(((bf16[80,3,16,128]{3,0,1,2:T(8,128)(2,1)}), bf16[80,3,16,128]{3,0,1,2:T(8,128)(2,1)S(1)}, u32[]{:S(2)}, u32[]{:S(2)}) %all-to-all-start) | async-done | bytes 983072 | tf_op jit(solution)/shard_map/all_to_all | solution.py:64
  146.4 0.1 copy.25
  146.5 1.4 collective-permute-start
  147.9 0.7 collective-permute-start.1
  148.6 0.0 copy-done.5
  148.6 0.6 dynamic_slice.37
  153.8 0.7 fusion.33
  163.3 0.8 dynamic_slice.48
  164.0 0.8 dynamic_slice.47
  164.8 0.0 copy-done
  164.8 0.7 gather_fusion.1
  165.5 0.7 gather_fusion.2
  170.6 0.7 gather_fusion.3
  171.2 0.1 broadcast_add_fusion
  171.3 1.7 broadcast_in_dim.51
  173.0 0.1 constant_dynamic-update-slice_fusion
  173.2 0.0 collective-permute-done
  173.2 1.4 collective-permute-start.2
  174.6 0.0 collective-permute-done.1
  174.6 0.7 collective-permute-start.3
  175.3 0.1 bitcast_dynamic-update-slice_fusion.6
  175.4 0.1 bitcast_dynamic-update-slice_fusion.5
  175.6 20.2 %collective-permute-done.2 = bf16[1280,3,128]{2,0,1:T(8,128)(2,1)S(1)} collective-permute-done((bf16[1280,3,128]{2,0,1:T(8,128)(2,1)S(1)}, bf16[1280,3,128]{2,0,1:T(8,128)(2,1)S(1)}, u32[]{:S(2)}, u32[]{:S(2)}) %collective-permute-start.2) | collective-permute-done | bytes 983072 | tf_op jit(solution)/shard_map/ppermute | solution.py:39
  195.7 1.3 collective-permute-start.4
  197.0 0.0 collective-permute-done.3
  197.0 0.7 collective-permute-start.5
  197.7 0.1 bitcast_dynamic-update-slice_fusion.4
  197.9 0.1 bitcast_dynamic-update-slice_fusion.3
  198.0 19.6 %collective-permute-done.4 = bf16[1280,3,128]{2,0,1:T(8,128)(2,1)S(1)} collective-permute-done((bf16[1280,3,128]{2,0,1:T(8,128)(2,1)S(1)}, bf16[1280,3,128]{2,0,1:T(8,128)(2,1)S(1)}, u32[]{:S(2)}, u32[]{:S(2)}) %collective-permute-start.4) | collective-permute-done | bytes 983072 | tf_op jit(solution)/shard_map/ppermute | solution.py:39
  217.6 1.3 collective-permute-start.6
  218.9 0.1 bitcast_dynamic-update-slice_fusion.2
  219.1 0.0 collective-permute-done.5
  219.1 0.1 bitcast_dynamic-update-slice_fusion.1
  219.2 19.2 %collective-permute-done.6 = bf16[1280,3,128]{2,0,1:T(8,128)(2,1)S(1)} collective-permute-done((bf16[1280,3,128]{2,0,1:T(8,128)(2,1)S(1)}, bf16[1280,3,128]{2,0,1:T(8,128)(2,1)S(1)}, u32[]{:S(2)}, u32[]{:S(2)}) %collective-permute-start.6) | collective-permute-done | bytes 983072 | tf_op jit(solution)/shard_map/ppermute | solution.py:39
  238.4 0.1 bitcast_dynamic-update-slice_fusion
  238.5 0.0 slice-start
  238.5 3.4 %constant_dynamic-slice_fusion.1 = (bf16[8,8,1,80,3,128]{5,3,2,1,4,0:T(8,128)(2,1)S(1)}, bf16[8,8,1,80,3,128]{5,3,2,1,4,0:T(8,128)(2,1)}) fusion(bf16[8,8,2,80,3,128]{5,3,2,1,4,0:T(8,128)(2,1)S(1)} %bitcast.115, s32[]{:T(128)S(6)} %select_n.160, s32[]{:T(128)S(6)} %select_n.162), kind=kLoop, calls=%fused_computation.40 | loop fusion | bytes 15728648 | tf_op jit(solution)/shard_map/jit(dynamic_index_in_dim)/dynamic_slice | solution.py:78
  241.9 0.0 collective-permute-done.7
  241.9 7.8 %fusion.15 = f32[3,128,3,256]{3,1,2,0:T(8,128)S(1)} fusion(bf16[8,8,80,3,256]{4,2,1,0,3:T(8,128)(2,1)} %bitcast.43, bf16[8,8,1,80,3,128]{5,3,2,1,4,0:T(8,128)(2,1)} %get-tuple-element.8), kind=kOutput, calls=%fused_computation.16 | convolution fusion | flops 3019898880 | bytes 12976128 | tf_op jit(solution)/shard_map/xrpia,rxpjb->ijab/dot_general | solution.py:80
  249.8 0.0 copy-start.1
  249.8 4.3 %fusion.25 = f32[3,3,256,128]{2,3,0,1:T(8,128)} fusion(f32[3,128,3,256]{3,1,2,0:T(8,128)S(1)} %fusion.15, bf16[8,8,80,3,256]{4,2,1,3,0:T(8,128)(2,1)S(1)} %bitcast.114, bf16[8,8,1,80,3,128]{5,3,2,1,4,0:T(8,128)(2,1)S(1)} %get-tuple-element.7), kind=kOutput, calls=%fused_computation.18 | convolution fusion | flops 3020193792 | bytes 14155776 | tf_op jit(solution)/shard_map/xrpia,rxpjb->ijab/dot_general | solution.py:75
  254.1 1.6 copy.33
  255.8 0.7 gather_fusion
  256.4 1.9 add_divide_fusion
  (15 shorter events, 0.0 us)
Async XLA Ops:
  0.0 164.8 %copy-start = (f32[300]{0:T(512)S(1)}, f32[300]{0:T(512)}, u32[]{:S(2)}) copy-start(f32[300]{0:T(512)} %param.10) | copy-start | bytes 3604
  119.0 5.4 %copy-start.3 = (bf16[8,640,3,256]{3,1,2,0:T(8,128)(2,1)}, bf16[8,640,3,256]{3,1,2,0:T(8,128)(2,1)S(1)}, u32[]{:S(2)}) copy-start(bf16[8,640,3,256]{3,1,2,0:T(8,128)(2,1)S(1)} %all_to_all.36) | copy-start | bytes 23592964
  119.0 5.4 %copy-start.4 = (bf16[80,3,2048]{2,0,1:T(8,128)(2,1)S(1)}, bf16[80,3,2048]{2,0,1:T(8,128)(2,1)}, u32[]{:S(2)}) copy-start(bf16[80,3,2048]{2,0,1:T(8,128)(2,1)} %param.9) | copy-start | bytes 2949124
  119.0 10.2 %copy-start.6 = (s32[3]{0:T(128)S(1)}, s32[3]{0:T(128)}, u32[]{:S(2)}) copy-start(s32[3]{0:T(128)} %param.12) | copy-start | bytes 40
  119.0 10.8 %copy-start.8 = (s32[16]{0:T(128)S(1)}, s32[16]{0:T(128)}, u32[]{:S(2)}) copy-start(s32[16]{0:T(128)} %param.14) | copy-start | bytes 196
  119.0 10.8 %copy-start.7 = (s32[16,2]{0,1:T(2,128)S(1)}, s32[16,2]{0,1:T(2,128)}, u32[]{:S(2)}) copy-start(s32[16,2]{0,1:T(2,128)} %param.13) | copy-start | bytes 388
  119.0 29.6 %copy-start.5 = (s32[8]{0:T(128)S(1)}, s32[8]{0:T(128)}, u32[]{:S(2)}) copy-start(s32[8]{0:T(128)} %constant.138.clone) | copy-start | bytes 100
  119.0 51.5 %copy-start.2 = (f32[4]{0:T(128)S(1)}, f32[4]{0:T(128)}, u32[]{:S(2)}) copy-start(f32[4]{0:T(128)} %param.15) | copy-start | bytes 52
  124.4 117.5 %collective-permute-start.7 = (bf16[5120,3,256]{2,0,1:T(8,128)(2,1)}, bf16[5120,3,256]{2,0,1:T(8,128)(2,1)}, u32[]{:S(2)}, u32[]{:S(2)}) collective-permute-start(bf16[5120,3,256]{2,0,1:T(8,128)(2,1)} %bitcast.117), channel_id=1, source_target_pairs={{0,1},{1,0},{2,3},{3,2},{4,5},{5,4},{6,7},{7,6},{8,9},{9,8},{10,11... | collective-permute-start | bytes 23592968 | tf_op jit(solution)/shard_map/ppermute | solution.py:63
  125.5 20.9 %all-to-all-start = ((bf16[80,3,16,128]{3,0,1,2:T(8,128)(2,1)}), bf16[80,3,16,128]{3,0,1,2:T(8,128)(2,1)S(1)}, u32[]{:S(2)}, u32[]{:S(2)}) async-start(bf16[80,3,16,128]{3,0,1,2:T(8,128)(2,1)} %copy_bitcast_fusion.1), calls=%async_computation | async-start | bytes 1966080 | tf_op jit(solution)/shard_map/all_to_all | solution.py:64
  146.5 26.7 %collective-permute-start = (bf16[1280,3,128]{2,0,1:T(8,128)(2,1)S(1)}, bf16[1280,3,128]{2,0,1:T(8,128)(2,1)S(1)}, u32[]{:S(2)}, u32[]{:S(2)}) collective-permute-start(bf16[1280,3,128]{2,0,1:T(8,128)(2,1)S(1)} %bitcast.119), channel_id=1, source_target_pairs={{0,16},{16,32},{32,48},{48,112},{112,96},{96,80},{80,64},{64,0},{1... | collective-permute-start | bytes 2949128 | tf_op jit(solution)/shard_map/ppermute | solution.py:39
  147.9 26.7 %collective-permute-start.1 = (bf16[1280,3,128]{2,0,1:T(8,128)(2,1)S(1)}, bf16[1280,3,128]{2,0,1:T(8,128)(2,1)S(1)}, u32[]{:S(2)}, u32[]{:S(2)}) collective-permute-start(bf16[1280,3,128]{2,0,1:T(8,128)(2,1)S(1)} %bitcast.120), channel_id=1, source_target_pairs={{0,64},{16,0},{32,16},{48,32},{112,48},{96,112},{80,96},{64,80},{1... | collective-permute-start | bytes 2949128 | tf_op jit(solution)/shard_map/ppermute | solution.py:42
  173.2 22.5 %collective-permute-start.2 = (bf16[1280,3,128]{2,0,1:T(8,128)(2,1)S(1)}, bf16[1280,3,128]{2,0,1:T(8,128)(2,1)S(1)}, u32[]{:S(2)}, u32[]{:S(2)}) collective-permute-start(bf16[1280,3,128]{2,0,1:T(8,128)(2,1)S(1)} %collective-permute-done), channel_id=1, source_target_pairs={{0,16},{16,32},{32,48},{48,112},{112,96},{96,80},{80,64},{64,0},{1... | collective-permute-start | bytes 2949128 | tf_op jit(solution)/shard_map/ppermute | solution.py:39
  174.6 22.4 %collective-permute-start.3 = (bf16[1280,3,128]{2,0,1:T(8,128)(2,1)S(1)}, bf16[1280,3,128]{2,0,1:T(8,128)(2,1)S(1)}, u32[]{:S(2)}, u32[]{:S(2)}) collective-permute-start(bf16[1280,3,128]{2,0,1:T(8,128)(2,1)S(1)} %collective-permute-done.1), channel_id=1, source_target_pairs={{0,64},{16,0},{32,16},{48,32},{112,48},{96,112},{80,96},{64,80},{1... | collective-permute-start | bytes 2949128 | tf_op jit(solution)/shard_map/ppermute | solution.py:42
  195.7 21.9 %collective-permute-start.4 = (bf16[1280,3,128]{2,0,1:T(8,128)(2,1)S(1)}, bf16[1280,3,128]{2,0,1:T(8,128)(2,1)S(1)}, u32[]{:S(2)}, u32[]{:S(2)}) collective-permute-start(bf16[1280,3,128]{2,0,1:T(8,128)(2,1)S(1)} %collective-permute-done.2), channel_id=1, source_target_pairs={{0,16},{16,32},{32,48},{48,112},{112,96},{96,80},{80,64},{64,0},{1... | collective-permute-start | bytes 2949128 | tf_op jit(solution)/shard_map/ppermute | solution.py:39
  197.0 22.1 %collective-permute-start.5 = (bf16[1280,3,128]{2,0,1:T(8,128)(2,1)S(1)}, bf16[1280,3,128]{2,0,1:T(8,128)(2,1)S(1)}, u32[]{:S(2)}, u32[]{:S(2)}) collective-permute-start(bf16[1280,3,128]{2,0,1:T(8,128)(2,1)S(1)} %collective-permute-done.3), channel_id=1, source_target_pairs={{0,64},{16,0},{32,16},{48,32},{112,48},{96,112},{80,96},{64,80},{1... | collective-permute-start | bytes 2949128 | tf_op jit(solution)/shard_map/ppermute | solution.py:42
  217.6 20.8 %collective-permute-start.6 = (bf16[1280,3,128]{2,0,1:T(8,128)(2,1)S(1)}, bf16[1280,3,128]{2,0,1:T(8,128)(2,1)S(1)}, u32[]{:S(2)}, u32[]{:S(2)}) collective-permute-start(bf16[1280,3,128]{2,0,1:T(8,128)(2,1)S(1)} %collective-permute-done.4), channel_id=1, source_target_pairs={{0,16},{16,32},{32,48},{48,112},{112,96},{96,80},{80,64},{64,0},{1... | collective-permute-start | bytes 2949128 | tf_op jit(solution)/shard_map/ppermute | solution.py:39
  238.5 11.2 %slice-start = ((s8[7864320]{0:T(1024)(128)(4,1)}), s8[3670016]{0:T(1024)(128)(4,1)S(1)}, s32[]{:S(2)}) async-start(s8[7864320]{0:T(1024)(128)(4,1)} %bitcast.112), calls=%async_computation.3 | async-start | bytes 7340032
  241.9 7.8 %slice-start.1 = ((s8[7864320]{0:T(1024)(128)(4,1)}), s8[4194304]{0:T(1024)(128)(4,1)S(1)}, s32[]{:S(2)}) async-start(s8[7864320]{0:T(1024)(128)(4,1)} %bitcast.112), calls=%async_computation.4 | async-start | bytes 8388608
  249.8 8.6 %copy-start.1 = (f32[300]{0:T(512)S(1)}, f32[300]{0:T(512)}, u32[]{:S(2)}) copy-start(f32[300]{0:T(512)} %param.10) | copy-start | bytes 3604
